TPU v7x, 32 devices: a whole 2x2x4 slice. The times are simulated.
32 devices in a mesh: space: 8 (over y, x, core), species: 4 (over z).
Axes of the slice: x: 2, y: 2, z: 4, core: 2. Of those that a mesh axis runs over, the one named last changes fastest.
Arguments:
- cotangent: bfloat16 [4, 400, 20, 1024], P('species', None, None, 'space'), may hold values from -6 to 6
- freq: float32 [4], P('species'), may hold values from 0.2 to 0.9
- ratio: float32 [4], P('species'), may hold values from 0.5 to 1
- coupling: float32 [4, 4, 13], replicated, may hold values from 0.1 to 0.6
- wall: int32 [1024], P('space'), may hold values 0 or 1
- inlet: int32 [1024], P('space'), may hold values 0 or 1
- face_type: int32 [2, 8], P(None, 'space'), may hold values from 0 to 1
Outputs:
- grad_state: bfloat16 [4, 400, 20, 1024], P('species', None, None, 'space')
Inputs may be any that keep to these rules, and one draw needn't show every extreme that they name: `wall`: 1 marks a solid cell. `inlet`: 1 marks an inlet cell. `face_type`: 0 is a specular wall, 1 a reversing wall.
All inputs are finite; a program needn't handle non-finite values. No bound on the sum of `wall` or of `inlet` on one device may be relied on, other than what follows from the above.
Results may differ from a plain program's by a relative error of at most 0.0049.
Values may be sent and summed in bfloat16 or wider, within the bound.
No kernel may reach another device: no remote copies, remote signals or barrier semaphores. Data moves between devices by JAX's collectives and lax.ppermute only.
A program may use at most 64 MiB of HBM per device.

v0:
```python
import math

import numpy as np
import jax
import jax.numpy as jnp
from jax import lax
from jax.experimental import pallas as pl
from jax.experimental.pallas import tpu as pltpu
from jax.sharding import PartitionSpec as P


NZ = 128

courant_max = 0.45
node_reach = 2.85


def passed_along(value, axis, steps):
    count = lax.axis_size(axis)
    pairs = [(source, (source + steps) % count) for source in range(count)]
    return lax.ppermute(value, axis, pairs)


def velocity_tables(node_count):
    pair_count = node_count * node_count
    spacing = 2.0 * node_reach / (node_count - 1)
    node_line = (np.arange(node_count, dtype=np.float64) - 0.5 * (node_count - 1)) * spacing
    grid_shape = (pair_count, node_count)
    along_x = np.broadcast_to(np.repeat(node_line, node_count)[:, None], grid_shape)
    along_y = np.broadcast_to(np.tile(node_line, node_count)[:, None], grid_shape)
    along_z = np.broadcast_to(node_line[None, :], grid_shape)
    square = along_x * along_x + along_y * along_y + along_z * along_z
    heat_term = square - 2.5
    functions = [
        np.ones(grid_shape),
        along_x,
        along_y,
        along_z,
        square - 1.5,
        along_x * along_y,
        along_x * along_z,
        along_y * along_z,
        along_x * along_x - along_y * along_y,
        along_y * along_y - along_z * along_z,
        along_x * heat_term,
        along_y * heat_term,
        along_z * heat_term,
    ]
    stacked = np.stack(functions)
    basis = stacked / np.sqrt(np.mean(stacked * stacked, axis=(1, 2), keepdims=True))
    weights = np.exp(-square) * (spacing * spacing * spacing) / math.pi**1.5
    recon = basis * weights[None]
    return node_line, basis, recon


def bf16_split(table, parts):
    rest = np.asarray(table, np.float64)
    pieces = []
    for _ in range(parts):
        piece = rest.astype(np.float32).astype(jnp.bfloat16).astype(np.float64)
        pieces.append(piece)
        rest = rest - piece
    return pieces


def on_device(cotangent, freq, ratio, coupling, wall, inlet, face_type):
    pair_count = cotangent.shape[1]
    node_count = cotangent.shape[2]
    cell_count = cotangent.shape[3]
    assert cell_count == NZ
    half = pair_count // 2
    moment_count = coupling.shape[2]
    species_count = lax.axis_size("species")

    node_line, basis, recon = velocity_tables(node_count)
    basis_k = np.transpose(basis, (0, 2, 1)).reshape(moment_count, node_count * pair_count)
    basis_parts = np.concatenate(bf16_split(basis_k, 3), axis=0)
    basis_parts = jnp.asarray(basis_parts.astype(jnp.bfloat16))
    weight_k = (recon[0] / basis[0]).T.reshape(-1).astype(np.float32)

    field_in = jnp.transpose(cotangent[0], (1, 0, 2))
    margin = (-half) % 16
    upper_in = field_in[:, half - margin :, :]
    lower_in = field_in[:, : half + margin, :]
    got_next = passed_along(upper_in, "space", -1)
    got_prev = passed_along(lower_in, "space", 1)

    open_cells = (1 - wall).astype(jnp.float32)
    keep_upper = open_cells * (1.0 - inlet.astype(jnp.float32))
    upward = (jnp.arange(pair_count) >= half)[None, :, None]
    keep = jnp.where(upward, keep_upper[None, None, :], open_cells[None, None, :])
    masked = field_in * keep.astype(jnp.bfloat16)
    parts = jnp.dot(
        basis_parts,
        masked.reshape(node_count * pair_count, cell_count),
        preferred_element_type=jnp.float32,
    )
    moments = parts[:moment_count] + parts[moment_count : 2 * moment_count] + parts[2 * moment_count :]

    species_index = lax.axis_index("species")
    row_k = lax.dynamic_index_in_dim(coupling, species_index, axis=0, keepdims=False)
    own_weight = lax.dynamic_index_in_dim(row_k, species_index, axis=0, keepdims=False)
    cross = own_weight[:, None] * moments
    for shift in range(1, species_count):
        source = (species_index - shift) % species_count
        other = passed_along(moments, "species", shift)
        weight = lax.dynamic_index_in_dim(row_k, source, axis=0, keepdims=False)
        cross = cross + weight[:, None] * other

    rows = 16
    assert moment_count + 2 < rows
    packet = jnp.concatenate(
        [
            cross,
            open_cells[None],
            keep_upper[None],
            jnp.zeros((rows - moment_count - 2, cell_count), jnp.float32),
        ],
        axis=0,
    )
    packet_next = passed_along(packet, "space", -1)
    packet_prev = passed_along(packet, "space", 1)

    rate_value = freq[0]
    scale_factor = courant_max * ratio[0] / node_reach
    line = jnp.asarray(node_line.astype(np.float32))
    pair_line = jnp.repeat(line, node_count)
    adv_x = jnp.abs(scale_factor * pair_line)
    adv_z = jnp.abs(scale_factor * line)
    columns = jnp.broadcast_to(
        jnp.stack([1.0 - adv_x, adv_x])[:, :, None], (2, pair_count, cell_count)
    )
    scalars = jnp.concatenate(
        [adv_z, jnp.zeros((31 - node_count,), jnp.float32), (1.0 - rate_value)[None]]
    )
    faces = face_type[:, 0]

    lanes = 128
    recon_halves = jnp.asarray(packed_recon(recon, rows, lanes))

    flip_rows = lax.broadcasted_iota(jnp.int32, (pair_count, pair_count), 0)
    flip_cols = lax.broadcasted_iota(jnp.int32, (pair_count, pair_count), 1)
    flip = (flip_rows + flip_cols == pair_count - 1).astype(jnp.bfloat16)

    partial = own_kernel(field_in, recon_halves, packet, columns, flip, scalars, faces)
    out = halo_kernel(
        partial, got_next, got_prev, recon_halves, packet_next, packet_prev,
        columns, scalars,
    )
    return jnp.transpose(out, (1, 0, 2))[None]


def packed_recon(recon, rows, lanes):
    moment_count, pair_count, node_count = recon.shape
    half = pair_count // 2
    table = np.transpose(recon, (2, 1, 0))
    parts = bf16_split(table, 2)
    order = [0, 0, 1]
    packed = np.zeros((node_count, half, lanes), np.float32)
    for side in range(2):
        for block, part in enumerate(order):
            at = side * (lanes // 2) + block * rows
            packed[:, :, at : at + moment_count] = parts[part][:, side * half : (side + 1) * half]
    return packed.astype(jnp.bfloat16)


def cross_matrix(packet, moment_count, side):
    rows, cells = packet.shape
    row = lax.broadcasted_iota(jnp.int32, packet.shape, 0)
    values = jnp.where(row < moment_count, packet, 0.0)
    c1 = values.astype(jnp.bfloat16)
    c2 = (values - c1.astype(jnp.float32)).astype(jnp.bfloat16)
    gap = jnp.zeros((64 - 3 * rows, cells), jnp.bfloat16)
    lead = jnp.zeros((64, cells), jnp.bfloat16)
    pieces = [c1, c2, c1, gap]
    return jnp.concatenate([lead] + pieces if side else pieces + [lead], axis=0)


def own_kernel(field_in, recon_halves, packet, columns, flip, scalars, faces):
    node_count, pair_count, cell_count = field_in.shape
    half = pair_count // 2
    steps = node_count // 2
    moment_count = packet.shape[0] - 3
    group = 5 if steps % 5 == 0 else 1
    blocks = steps // group

    def kernel(sc_ref, face_ref, cot_lo, cot_hi, rec_lo, rec_hi, pk_ref, col_ref, flip_ref, out_ref):
        b = pl.program_id(0)
        row = lax.broadcasted_iota(jnp.int32, (pair_count, cell_count), 0)
        lane = lax.broadcasted_iota(jnp.int32, (pair_count, cell_count), 1)
        pk = pk_ref[...]
        rate = sc_ref[31]
        keep = rate * jnp.where(row >= half, pk[moment_count + 1 : moment_count + 2, :], pk[moment_count : moment_count + 1, :])
        own_lo = cross_matrix(pk, moment_count, 0)
        own_hi = cross_matrix(pk, moment_count, 1)
        base = col_ref[0]
        face_a = face_ref[0] == 1
        face_b = face_ref[1] == 1

        def relax(values, rec_ref, at):
            rec = rec_ref[at]
            rebuilt = jnp.concatenate(
                [
                    jnp.dot(rec, own_lo, preferred_element_type=jnp.float32),
                    jnp.dot(rec, own_hi, preferred_element_type=jnp.float32),
                ],
                axis=0,
            )
            return (keep * values.astype(jnp.float32) + rebuilt).astype(jnp.bfloat16)

        def one(t, carry):
            u = group - 1 - t
            j = b * group + t
            relaxed_a = relax(cot_lo[t], rec_lo, t)
            relaxed_b = relax(cot_hi[u], rec_hi, u)
            edges = jnp.where(lane == 0, relaxed_b, relaxed_a)
            flipped = jnp.dot(flip_ref[...], edges, preferred_element_type=jnp.float32)
            edges32 = edges.astype(jnp.float32)
            source_a = jnp.where(face_a, flipped, edges32)
            source_b = jnp.where(face_b, flipped, edges32)
            ra = relaxed_a.astype(jnp.float32)
            rb = relaxed_b.astype(jnp.float32)
            near_a = jnp.where(lane == 0, source_a, pltpu.roll(ra, 1, 1))
            near_b = jnp.where(lane == cell_count - 1, source_b, pltpu.roll(rb, cell_count - 1, 1))
            zw_a = sc_ref[j]
            zw_b = sc_ref[node_count - 1 - j]
            out_ref[0, t] = (base - zw_a) * ra + zw_a * near_a
            out_ref[1, t] = (base - zw_b) * rb + zw_b * near_b
            return carry

        lax.fori_loop(0, group, one, 0)

    block = (group, pair_count, cell_count)
    smem = pl.BlockSpec(memory_space=pltpu.SMEM)
    in_specs = [
        smem,
        smem,
        pl.BlockSpec(block, lambda b: (b, 0, 0)),
        pl.BlockSpec(block, lambda b: (2 * blocks - 1 - b, 0, 0)),
        pl.BlockSpec((group, half, recon_halves.shape[2]), lambda b: (b, 0, 0)),
        pl.BlockSpec((group, half, recon_halves.shape[2]), lambda b: (2 * blocks - 1 - b, 0, 0)),
        pl.BlockSpec(packet.shape, lambda b: (0, 0)),
        pl.BlockSpec((1, pair_count, cell_count), lambda b: (0, 0, 0)),
        pl.BlockSpec(flip.shape, lambda b: (0, 0)),
    ]
    return pl.pallas_call(
        kernel,
        grid=(blocks,),
        in_specs=in_specs,
        out_specs=pl.BlockSpec((2,) + block, lambda b: (0, b, 0, 0)),
        out_shape=jax.ShapeDtypeStruct((2, steps, pair_count, cell_count), jnp.float32),
        compiler_params=pltpu.CompilerParams(
            dimension_semantics=("arbitrary",), vmem_limit_bytes=48 * 1024 * 1024
        ),
    )(scalars, faces, field_in, field_in, recon_halves, recon_halves, packet, columns, flip)


def halo_kernel(partial, got_next, got_prev, recon_halves, packet_next, packet_prev, columns, scalars):
    node_count, wide, cell_count = got_next.shape
    half = recon_halves.shape[1]
    margin = wide - half
    pair_count = 2 * half
    steps = node_count // 2
    moment_count = packet_next.shape[0] - 3
    group = 5 if steps % 5 == 0 else 1
    blocks = node_count // group
    lower_blocks = steps // group

    def kernel(sc_ref, part_ref, nxt_ref, prv_ref, rec_ref, pn_ref, pp_ref, col_ref, out_ref):
        i = pl.program_id(0)
        rate = sc_ref[31]
        pn = pn_ref[...]
        pp = pp_ref[...]
        next_mat = cross_matrix(pn, moment_count, 1)
        prev_mat = cross_matrix(pp, moment_count, 0)
        keep_up = rate * pn[moment_count + 1 : moment_count + 2, :]
        keep_down = rate * pp[moment_count : moment_count + 1, :]
        side = col_ref[0]

        def run(mirrored):
            def one(t, carry):
                rec = rec_ref[t]
                up = jnp.dot(rec, next_mat, preferred_element_type=jnp.float32)
                down = jnp.dot(rec, prev_mat, preferred_element_type=jnp.float32)
                nxt = nxt_ref[t].astype(jnp.float32)[margin:]
                prv = prv_ref[t].astype(jnp.float32)[:half]
                up = (keep_up * nxt + up).astype(jnp.bfloat16)
                down = (keep_down * prv + down).astype(jnp.bfloat16)
                shifted = jnp.concatenate([down.astype(jnp.float32), up.astype(jnp.float32)], axis=0)
                part = part_ref[0, group - 1 - t] if mirrored else part_ref[0, t]
                out_ref[t] = (part + side * shifted).astype(jnp.bfloat16)
                return carry

            lax.fori_loop(0, group, one, 0)

        @pl.when(i < lower_blocks)
        def _():
            run(False)

        @pl.when(i >= lower_blocks)
        def _():
            run(True)

    block = (group, pair_count, cell_count)
    smem = pl.BlockSpec(memory_space=pltpu.SMEM)
    in_specs = [
        smem,
        pl.BlockSpec(
            (1,) + block,
            lambda i: (
                jnp.where(i < lower_blocks, 0, 1),
                jnp.where(i < lower_blocks, i, blocks - 1 - i),
                0,
                0,
            ),
        ),
        pl.BlockSpec((group, wide, cell_count), lambda i: (i, 0, 0)),
        pl.BlockSpec((group, wide, cell_count), lambda i: (i, 0, 0)),
        pl.BlockSpec((group, half, recon_halves.shape[2]), lambda i: (i, 0, 0)),
        pl.BlockSpec(packet_next.shape, lambda i: (0, 0)),
        pl.BlockSpec(packet_prev.shape, lambda i: (0, 0)),
        pl.BlockSpec((1, pair_count, cell_count), lambda i: (1, 0, 0)),
    ]
    return pl.pallas_call(
        kernel,
        grid=(blocks,),
        in_specs=in_specs,
        out_specs=pl.BlockSpec(block, lambda i: (i, 0, 0)),
        out_shape=jax.ShapeDtypeStruct((node_count, pair_count, cell_count), jnp.bfloat16),
        compiler_params=pltpu.CompilerParams(
            dimension_semantics=("arbitrary",), vmem_limit_bytes=48 * 1024 * 1024
        ),
    )(scalars, partial, got_next, got_prev, recon_halves, packet_next, packet_prev, columns)


def solution(mesh):
    in_specs = (
        P("species", None, None, "space"),
        P("species"),
        P("species"),
        P(),
        P("space"),
        P("space"),
        P(None, "space"),
    )
    out_specs = P("species", None, None, "space")

    return jax.shard_map(on_device, mesh=mesh, in_specs=in_specs, out_specs=out_specs, check_vma=False)
```

profile of v0, /device:TPU:1, one launch (start us, length us, event | category | flops | bytes accessed | tf_op | source)
XLA Modules:
  0.0 46.7 jit_solution(14020824979210284813)
XLA Ops:
  0.0 0.7 %subtract_convert_fusion = (bf16[128]{0:T(256)(128)(2,1)S(1)}, f32[1,128]{1,0:T(1,128)S(1)}) fusion(s32[128]{0:T(128)} %param.14), kind=kLoop, calls=%fused_computation.21 | loop fusion | flops 384 | bytes 1280 | tf_op jit(solution)/shard_map/convert_element_type | solution.py:88
  0.7 0.7 %subtract_multiply_fusion = f32[128]{0:T(128)S(1)} fusion(s32[128]{0:T(128)} %param.15, s32[128]{0:T(128)} %param.14), kind=kLoop, calls=%fused_computation.20 | loop fusion | flops 640 | bytes 1536 | tf_op jit(solution)/shard_map/mul | solution.py:89
  1.3 0.1 select_convert_fusion
  1.5 0.0 copy-start.3
  1.5 1.8 %broadcast_multiply_fusion = bf16[20,400,128]{2,1,0:T(8,128)(2,1)S(1)} fusion(bf16[400,128]{1,0:T(8,128)(2,1)S(1)} %select_convert_fusion, bf16[1,400,20,128]{3,1,2,0:T(8,128)(2,1)} %param.10), kind=kLoop, calls=%fused_computation | loop fusion | flops 1024000 | bytes 4198400 | tf_op jit(solution)/shard_map/mul | solution.py:92
  3.3 0.0 copy-start
  3.3 0.0 copy-done.3
  3.3 0.5 %fusion.7 = f32[39,128]{1,0:T(8,128)S(1)} fusion(bf16[39,8000]{1,0:T(8,128)(2,1)S(1)} %copy-done.3, bf16[8000,128]{1,0:T(8,128)(2,1)S(1)} %bitcast.28), kind=kOutput, calls=%fused_computation.25 | convolution fusion | flops 79872000 | bytes 2691968 | tf_op jit(solution)/shard_map/dot_general | solution.py:93
  3.8 3.2 %collective-permute-start.1 = (f32[13,128]{1,0:T(8,128)S(1)}, f32[13,128]{1,0:T(8,128)S(1)}, u32[]{:S(2)}, u32[]{:S(2)}) collective-permute-start(f32[13,128]{1,0:T(8,128)S(1)} %slice_add_fusion), channel_id=1, source_target_pairs={{0,2},{1,3},{2,0},{3,1},{4,6},{5,7},{6,4},{7,5},{8,10},{9,11},{10,... | collective-permute-start | bytes 19976 | tf_op jit(solution)/shard_map/ppermute | solution.py:21
  7.0 1.3 %collective-permute-start = (f32[13,128]{1,0:T(8,128)S(1)}, f32[13,128]{1,0:T(8,128)S(1)}, u32[]{:S(2)}, u32[]{:S(2)}) collective-permute-start(f32[13,128]{1,0:T(8,128)S(1)} %slice_add_fusion), channel_id=1, source_target_pairs={{0,1},{1,2},{2,3},{3,0},{4,5},{5,6},{6,7},{7,4},{8,9},{9,10},{10,1... | collective-permute-start | bytes 19976 | tf_op jit(solution)/shard_map/ppermute | solution.py:21
  8.3 2.0 %collective-permute-start.2 = (f32[13,128]{1,0:T(8,128)S(1)}, f32[13,128]{1,0:T(8,128)S(1)}, u32[]{:S(2)}, u32[]{:S(2)}) collective-permute-start(f32[13,128]{1,0:T(8,128)S(1)} %slice_add_fusion), channel_id=1, source_target_pairs={{0,3},{1,0},{2,1},{3,2},{4,7},{5,4},{6,5},{7,6},{8,11},{9,8},{10,9... | collective-permute-start | bytes 19976 | tf_op jit(solution)/shard_map/ppermute | solution.py:21
  10.3 0.0 copy-done
  10.3 0.0 copy-start.4
  10.3 0.0 copy-start.1
  10.3 0.0 copy-start.2
  10.3 1.5 %fusion.6 = (bf16[20,208,128]{2,1,0:T(8,128)(2,1)}, bf16[20,208,128]{2,1,0:T(8,128)(2,1)}) fusion(bf16[20,400,128]{2,1,0:T(8,128)(2,1)S(1)} %bitcast.24), kind=kLoop, calls=%fused_computation.24 | loop fusion | bytes 4259840 | tf_op jit(solution)/shard_map/slice | solution.py:84
  11.8 2.6 %collective-permute-start.4 = (bf16[20,208,128]{2,1,0:T(8,128)(2,1)}, bf16[20,208,128]{2,1,0:T(8,128)(2,1)}, u32[]{:S(2)}, u32[]{:S(2)}) collective-permute-start(bf16[20,208,128]{2,1,0:T(8,128)(2,1)} %get-tuple-element.5), channel_id=1, source_target_pairs={{0,4},{4,8},{8,12},{12,16},{16,20},{20,24},{24,28},{28,0},{1,5},{5... | collective-permute-start | bytes 3194888 | tf_op jit(solution)/shard_map/ppermute | solution.py:21
  14.4 0.0 collective-permute-start.3
  15.0 0.0 copy-done.4
  15.0 0.1 broadcast_in_dim.59
  15.1 0.1 abs.20
  15.3 0.8 %fusion.1 = (f32[13]{0:T(128)S(1)}, f32[13]{0:T(128)S(1)}, f32[13]{0:T(128)S(1)}, f32[13]{0:T(128)S(1)}) fusion(f32[4,4,13]{2,1,0:T(4,128)} %param.13, s32[]{:T(128)S(6)} %select_n.48, s32[]{:T(128)S(6)} %select_n.52, s32[]{:T(128)S(6)} %select_n.58, s32[]{:T(128)S(6)} %select_n.55), kind=kLoop, calls=%fused_computation.15 | loop fusion | bytes 432 | tf_op jit(solution)/shard_map/mul | solution.py:103
  16.8 0.1 pad.5.clone
  16.9 0.0 collective-permute-done.1
  16.9 0.0 collective-permute-done
  16.9 0.0 collective-permute-done.2
  16.9 0.1 multiply_add_fusion
  17.0 0.1 maximum_maximum_fusion.pk_ref
  17.0 1.7 %collective-permute-start.6 = (f32[16,128]{1,0:T(8,128)S(1)}, f32[16,128]{1,0:T(8,128)S(1)}, u32[]{:S(2)}, u32[]{:S(2)}) collective-permute-start(f32[16,128]{1,0:T(8,128)S(1)} %maximum_maximum_fusion.pk_ref), channel_id=1, source_target_pairs={{0,4},{4,8},{8,12},{12,16},{16,20},{20,24},{24,28},{28,0},{1,5},{5... | collective-permute-start | bytes 24584 | tf_op jit(solution)/shard_map/ppermute | solution.py:21
  18.8 0.0 collective-permute-start.5
  18.8 0.1 pad_maximum_fusion.1.sc_ref
  18.9 0.2 broadcast_in_dim.60.col_ref
  19.0 0.0 copy-done.1
  19.0 0.0 copy-done.2
  19.0 7.0 %shard_map.100.part_ref = f32[2,10,400,128]{3,2,1,0:T(8,128)} custom-call(f32[32]{0:T(128)S(1)} %pad_maximum_fusion.1.sc_ref, s32[2]{0:T(128)S(1)} %bitcast.27, bf16[20,400,128]{2,1,0:T(8,128)(2,1)S(1)} %bitcast.25, bf16[20,400,128]{2,1,0:T(8,128)(2,1)S(1)} %bitcast.26, bf16[20,200,128]{2,1,0:T(8,128)(2,1)S(1)} %copy-done.1, ...), custom_call_target="tpu_custom_call" | custom-call | tf_op jit(solution)/shard_map/pallas_call | solution.py:246
  26.0 10.3 %collective-permute-done.6.pp_ref = f32[16,128]{1,0:T(8,128)S(1)} collective-permute-done((f32[16,128]{1,0:T(8,128)S(1)}, f32[16,128]{1,0:T(8,128)S(1)}, u32[]{:S(2)}, u32[]{:S(2)}) %collective-permute-start.6) | collective-permute-done | bytes 8224 | tf_op jit(solution)/shard_map/ppermute | solution.py:21
  36.3 3.4 %collective-permute-done.5.pn_ref = f32[16,128]{1,0:T(8,128)S(1)} collective-permute-done((f32[16,128]{1,0:T(8,128)S(1)}, f32[16,128]{1,0:T(8,128)S(1)}, u32[]{:S(2)}, u32[]{:S(2)}) %collective-permute-start.5) | collective-permute-done | bytes 8224 | tf_op jit(solution)/shard_map/ppermute | solution.py:21
  39.8 0.0 collective-permute-done.4.prv_ref
  39.8 0.0 collective-permute-done.3.nxt_ref
  39.8 6.9 %shard_map.101 = bf16[20,400,128]{2,1,0:T(8,128)(2,1)} custom-call(f32[32]{0:T(128)S(1)} %pad_maximum_fusion.1.sc_ref, f32[2,10,400,128]{3,2,1,0:T(8,128)} %shard_map.100.part_ref, bf16[20,208,128]{2,1,0:T(8,128)(2,1)} %collective-permute-done.3.nxt_ref, bf16[20,208,128]{2,1,0:T(8,128)(2,1)} %collective-permute-done.4.prv_ref, ...), custom_call_target="tpu_custom_call" | custom-call | tf_op jit(solution)/shard_map/pallas_call | solution.py:324
  (7 shorter events, 0.1 us)
Async XLA Ops:
  1.5 1.8 %copy-start.3 = (bf16[39,8000]{1,0:T(8,128)(2,1)S(1)}, bf16[39,8000]{1,0:T(8,128)(2,1)}, u32[]{:S(2)}) copy-start(bf16[39,8000]{1,0:T(8,128)(2,1)} %constant.139.clone) | copy-start | bytes 1872004
  3.3 7.0 %copy-start = (bf16[1,400,20,128]{3,1,2,0:T(8,128)(2,1)S(1)}, bf16[1,400,20,128]{3,1,2,0:T(8,128)(2,1)}, u32[]{:S(2)}) copy-start(bf16[1,400,20,128]{3,1,2,0:T(8,128)(2,1)} %param.10) | copy-start | bytes 6144004
  3.8 13.0 %collective-permute-start.1 = (f32[13,128]{1,0:T(8,128)S(1)}, f32[13,128]{1,0:T(8,128)S(1)}, u32[]{:S(2)}, u32[]{:S(2)}) collective-permute-start(f32[13,128]{1,0:T(8,128)S(1)} %slice_add_fusion), channel_id=1, source_target_pairs={{0,2},{1,3},{2,0},{3,1},{4,6},{5,7},{6,4},{7,5},{8,10},{9,11},{10,... | collective-permute-start | bytes 19976 | tf_op jit(solution)/shard_map/ppermute | solution.py:21
  7.0 9.8 %collective-permute-start = (f32[13,128]{1,0:T(8,128)S(1)}, f32[13,128]{1,0:T(8,128)S(1)}, u32[]{:S(2)}, u32[]{:S(2)}) collective-permute-start(f32[13,128]{1,0:T(8,128)S(1)} %slice_add_fusion), channel_id=1, source_target_pairs={{0,1},{1,2},{2,3},{3,0},{4,5},{5,6},{6,7},{7,4},{8,9},{9,10},{10,1... | collective-permute-start | bytes 19976 | tf_op jit(solution)/shard_map/ppermute | solution.py:21
  8.3 8.6 %collective-permute-start.2 = (f32[13,128]{1,0:T(8,128)S(1)}, f32[13,128]{1,0:T(8,128)S(1)}, u32[]{:S(2)}, u32[]{:S(2)}) collective-permute-start(f32[13,128]{1,0:T(8,128)S(1)} %slice_add_fusion), channel_id=1, source_target_pairs={{0,3},{1,0},{2,1},{3,2},{4,7},{5,4},{6,5},{7,6},{8,11},{9,8},{10,9... | collective-permute-start | bytes 19976 | tf_op jit(solution)/shard_map/ppermute | solution.py:21
  10.3 4.7 %copy-start.4 = (f32[20]{0:T(128)S(1)}, f32[20]{0:T(128)}, u32[]{:S(2)}) copy-start(f32[20]{0:T(128)} %constant.140.clone) | copy-start | bytes 244
  10.3 8.7 %copy-start.1 = (bf16[20,200,128]{2,1,0:T(8,128)(2,1)S(1)}, bf16[20,200,128]{2,1,0:T(8,128)(2,1)}, u32[]{:S(2)}) copy-start(bf16[20,200,128]{2,1,0:T(8,128)(2,1)} %constant.141.clone.rec_lo.rec_hi.rec_ref) | copy-start | bytes 3072004
  10.3 8.7 %copy-start.2 = (s32[2,1]{0,1:T(1,128)S(1)}, s32[2,1]{0,1:T(1,128)}, u32[]{:S(2)}) copy-start(s32[2,1]{0,1:T(1,128)} %param.16) | copy-start | bytes 28
  11.8 28.0 %collective-permute-start.4 = (bf16[20,208,128]{2,1,0:T(8,128)(2,1)}, bf16[20,208,128]{2,1,0:T(8,128)(2,1)}, u32[]{:S(2)}, u32[]{:S(2)}) collective-permute-start(bf16[20,208,128]{2,1,0:T(8,128)(2,1)} %get-tuple-element.5), channel_id=1, source_target_pairs={{0,4},{4,8},{8,12},{12,16},{16,20},{20,24},{24,28},{28,0},{1,5},{5... | collective-permute-start | bytes 3194888 | tf_op jit(solution)/shard_map/ppermute | solution.py:21
  14.4 25.4 %collective-permute-start.3 = (bf16[20,208,128]{2,1,0:T(8,128)(2,1)}, bf16[20,208,128]{2,1,0:T(8,128)(2,1)}, u32[]{:S(2)}, u32[]{:S(2)}) collective-permute-start(bf16[20,208,128]{2,1,0:T(8,128)(2,1)} %get-tuple-element.6), channel_id=1, source_target_pairs={{0,28},{4,0},{8,4},{12,8},{16,12},{20,16},{24,20},{28,24},{1,29},{... | collective-permute-start | bytes 3194888 | tf_op jit(solution)/shard_map/ppermute | solution.py:21
  17.0 19.3 %collective-permute-start.6 = (f32[16,128]{1,0:T(8,128)S(1)}, f32[16,128]{1,0:T(8,128)S(1)}, u32[]{:S(2)}, u32[]{:S(2)}) collective-permute-start(f32[16,128]{1,0:T(8,128)S(1)} %maximum_maximum_fusion.pk_ref), channel_id=1, source_target_pairs={{0,4},{4,8},{8,12},{12,16},{16,20},{20,24},{24,28},{28,0},{1,5},{5... | collective-permute-start | bytes 24584 | tf_op jit(solution)/shard_map/ppermute | solution.py:21
  18.8 21.0 %collective-permute-start.5 = (f32[16,128]{1,0:T(8,128)S(1)}, f32[16,128]{1,0:T(8,128)S(1)}, u32[]{:S(2)}, u32[]{:S(2)}) collective-permute-start(f32[16,128]{1,0:T(8,128)S(1)} %maximum_maximum_fusion.pk_ref), channel_id=1, source_target_pairs={{0,28},{4,0},{8,4},{12,8},{16,12},{20,16},{24,20},{28,24},{1,29},{... | collective-permute-start | bytes 24584 | tf_op jit(solution)/shard_map/ppermute | solution.py:21
where the time goes:
time: 47 us; the launch traced here: 46.7 us
  Pallas kernels  13.9 us (30%)
  waiting for transfers between devices  13.7 us (29%)
  starting transfers between devices  10.8 us (23%)
  other arithmetic  3.57 us (8%)
  local copies, waits for them, and re-layouts  2.73 us (6%)
  between operations  1.44 us (3%)
  matrix products  0.5 us (1%)
    ppermute x7, waiting for transfers between devices, passed_along(): return lax.ppermute(value, axis, pairs)  13.7 us
    ppermute x7, starting transfers between devices, passed_along(): return lax.ppermute(value, axis, pairs)  10.8 us
    pallas_call x1, Pallas kernels, own_kernel(): pl.pallas_call(kernel, grid=(blocks,), in_specs=in_specs, out_specs=pl.Bl...  6.98 us
    pallas_call x1, Pallas kernels, halo_kernel(): pl.pallas_call(kernel, grid=(blocks,), in_specs=in_specs, out_specs=pl.Bl...  6.95 us
    mul x1, other arithmetic, on_device(): masked = field_in * keep.astype(jnp.bfloat16)  1.81 us
    slice x1, local copies, waits for them, and re-layouts, on_device(): lower_in = field_in[:, :half + margin, :]  1.46 us
  transfers between devices with their start and end apart: 7, of which 2 were waited for; matrix products, arithmetic and copies ran while one was open for 6% of the time, Pallas kernels for 15%

commit v1 on v0

--- a/solution.py
+++ b/solution.py
@@ -191,21 +191,16 @@
         pk = pk_ref[...]
         rate = sc_ref[31]
         keep = rate * jnp.where(row >= half, pk[moment_count + 1 : moment_count + 2, :], pk[moment_count : moment_count + 1, :])
-        own_lo = cross_matrix(pk, moment_count, 0)
-        own_hi = cross_matrix(pk, moment_count, 1)
+        own_both = jnp.concatenate(
+            [cross_matrix(pk, moment_count, 0), cross_matrix(pk, moment_count, 1)], axis=1
+        )
         base = col_ref[0]
         face_a = face_ref[0] == 1
         face_b = face_ref[1] == 1
 
         def relax(values, rec_ref, at):
-            rec = rec_ref[at]
-            rebuilt = jnp.concatenate(
-                [
-                    jnp.dot(rec, own_lo, preferred_element_type=jnp.float32),
-                    jnp.dot(rec, own_hi, preferred_element_type=jnp.float32),
-                ],
-                axis=0,
-            )
+            both = jnp.dot(rec_ref[at], own_both, preferred_element_type=jnp.float32)
+            rebuilt = jnp.concatenate([both[:, :cell_count], both[:, cell_count:]], axis=0)
             return (keep * values.astype(jnp.float32) + rebuilt).astype(jnp.bfloat16)
 
         def one(t, carry):
@@ -271,17 +266,18 @@
         rate = sc_ref[31]
         pn = pn_ref[...]
         pp = pp_ref[...]
-        next_mat = cross_matrix(pn, moment_count, 1)
-        prev_mat = cross_matrix(pp, moment_count, 0)
+        halo_mats = jnp.concatenate(
+            [cross_matrix(pn, moment_count, 1), cross_matrix(pp, moment_count, 0)], axis=1
+        )
         keep_up = rate * pn[moment_count + 1 : moment_count + 2, :]
         keep_down = rate * pp[moment_count : moment_count + 1, :]
         side = col_ref[0]
 
         def run(mirrored):
             def one(t, carry):
-                rec = rec_ref[t]
-                up = jnp.dot(rec, next_mat, preferred_element_type=jnp.float32)
-                down = jnp.dot(rec, prev_mat, preferred_element_type=jnp.float32)
+                both = jnp.dot(rec_ref[t], halo_mats, preferred_element_type=jnp.float32)
+                up = both[:, :cell_count]
+                down = both[:, cell_count:]
                 nxt = nxt_ref[t].astype(jnp.float32)[margin:]
                 prv = prv_ref[t].astype(jnp.float32)[:half]
                 up = (keep_up * nxt + up).astype(jnp.bfloat16)

time: 47 us -> 46.7 us (level)
  Pallas kernels: 13.9 us -> 13.1 us
  waiting for transfers between devices: 13.7 us -> 14.2 us
    pallas_call x1, Pallas kernels: 6.98 us -> 6.47 us  [own_kernel(): pl.pallas_call(kernel, grid=(blocks,), in_specs=in_specs, out_specs=pl.Bl...]
    ppermute x7, waiting for transfers between devices: 13.7 us -> 14.2 us  [passed_along(): return lax.ppermute(value, axis, pairs)]
  transfers between devices with their start and end apart: 7 -> 7, of which waited for: 2 -> 2; matrix products, arithmetic and copies ran while one was open for 6% -> 6% of each run, Pallas kernels for 15% -> 14%
where the time goes in v1:
time: 46.7 us; the launch traced here: 46.4 us
  waiting for transfers between devices  14.2 us (30%)
  Pallas kernels  13.1 us (28%)
  starting transfers between devices  10.8 us (23%)
  other arithmetic  3.57 us (8%)
  local copies, waits for them, and re-layouts  2.73 us (6%)
  between operations  1.44 us (3%)
  matrix products  0.5 us (1%)
    ppermute x7, waiting for transfers between devices, passed_along(): return lax.ppermute(value, axis, pairs)  14.2 us
    ppermute x7, starting transfers between devices, passed_along(): return lax.ppermute(value, axis, pairs)  10.8 us
    pallas_call x1, Pallas kernels, halo_kernel(): pl.pallas_call(kernel, grid=(blocks,), in_specs=in_specs, out_specs=pl.Bl...  6.67 us
    pallas_call x1, Pallas kernels, own_kernel(): pl.pallas_call(kernel, grid=(blocks,), in_specs=in_specs, out_specs=pl.Bl...  6.47 us
    mul x1, other arithmetic, on_device(): masked = field_in * keep.astype(jnp.bfloat16)  1.81 us
    slice x1, local copies, waits for them, and re-layouts, on_device(): lower_in = field_in[:, :half + margin, :]  1.46 us
  transfers between devices with their start and end apart: 7, of which 2 were waited for; matrix products, arithmetic and copies ran while one was open for 6% of the time, Pallas kernels for 14%

profile of v1, /device:TPU:1, one launch (start us, length us, event | category | flops | bytes accessed | tf_op | source)
XLA Modules:
  0.0 46.4 jit_solution(9194258792210702968)
XLA Ops:
  0.0 0.7 %subtract_convert_fusion = (bf16[128]{0:T(256)(128)(2,1)S(1)}, f32[1,128]{1,0:T(1,128)S(1)}) fusion(s32[128]{0:T(128)} %param.14), kind=kLoop, calls=%fused_computation.21 | loop fusion | flops 384 | bytes 1280 | tf_op jit(solution)/shard_map/convert_element_type | solution.py:88
  0.7 0.7 %subtract_multiply_fusion = f32[128]{0:T(128)S(1)} fusion(s32[128]{0:T(128)} %param.15, s32[128]{0:T(128)} %param.14), kind=kLoop, calls=%fused_computation.20 | loop fusion | flops 640 | bytes 1536 | tf_op jit(solution)/shard_map/mul | solution.py:89
  1.3 0.1 select_convert_fusion
  1.5 0.0 copy-start.3
  1.5 1.8 %broadcast_multiply_fusion = bf16[20,400,128]{2,1,0:T(8,128)(2,1)S(1)} fusion(bf16[400,128]{1,0:T(8,128)(2,1)S(1)} %select_convert_fusion, bf16[1,400,20,128]{3,1,2,0:T(8,128)(2,1)} %param.10), kind=kLoop, calls=%fused_computation | loop fusion | flops 1024000 | bytes 4198400 | tf_op jit(solution)/shard_map/mul | solution.py:92
  3.3 0.0 copy-start
  3.3 0.0 copy-done.3
  3.3 0.5 %fusion.7 = f32[39,128]{1,0:T(8,128)S(1)} fusion(bf16[39,8000]{1,0:T(8,128)(2,1)S(1)} %copy-done.3, bf16[8000,128]{1,0:T(8,128)(2,1)S(1)} %bitcast.28), kind=kOutput, calls=%fused_computation.25 | convolution fusion | flops 79872000 | bytes 2691968 | tf_op jit(solution)/shard_map/dot_general | solution.py:93
  3.8 3.2 %collective-permute-start.1 = (f32[13,128]{1,0:T(8,128)S(1)}, f32[13,128]{1,0:T(8,128)S(1)}, u32[]{:S(2)}, u32[]{:S(2)}) collective-permute-start(f32[13,128]{1,0:T(8,128)S(1)} %slice_add_fusion), channel_id=1, source_target_pairs={{0,2},{1,3},{2,0},{3,1},{4,6},{5,7},{6,4},{7,5},{8,10},{9,11},{10,... | collective-permute-start | bytes 19976 | tf_op jit(solution)/shard_map/ppermute | solution.py:21
  7.0 1.3 %collective-permute-start = (f32[13,128]{1,0:T(8,128)S(1)}, f32[13,128]{1,0:T(8,128)S(1)}, u32[]{:S(2)}, u32[]{:S(2)}) collective-permute-start(f32[13,128]{1,0:T(8,128)S(1)} %slice_add_fusion), channel_id=1, source_target_pairs={{0,1},{1,2},{2,3},{3,0},{4,5},{5,6},{6,7},{7,4},{8,9},{9,10},{10,1... | collective-permute-start | bytes 19976 | tf_op jit(solution)/shard_map/ppermute | solution.py:21
  8.3 2.0 %collective-permute-start.2 = (f32[13,128]{1,0:T(8,128)S(1)}, f32[13,128]{1,0:T(8,128)S(1)}, u32[]{:S(2)}, u32[]{:S(2)}) collective-permute-start(f32[13,128]{1,0:T(8,128)S(1)} %slice_add_fusion), channel_id=1, source_target_pairs={{0,3},{1,0},{2,1},{3,2},{4,7},{5,4},{6,5},{7,6},{8,11},{9,8},{10,9... | collective-permute-start | bytes 19976 | tf_op jit(solution)/shard_map/ppermute | solution.py:21
  10.3 0.0 copy-done
  10.3 0.0 copy-start.4
  10.3 0.0 copy-start.1
  10.3 0.0 copy-start.2
  10.3 1.5 %fusion.6 = (bf16[20,208,128]{2,1,0:T(8,128)(2,1)}, bf16[20,208,128]{2,1,0:T(8,128)(2,1)}) fusion(bf16[20,400,128]{2,1,0:T(8,128)(2,1)S(1)} %bitcast.24), kind=kLoop, calls=%fused_computation.24 | loop fusion | bytes 4259840 | tf_op jit(solution)/shard_map/slice | solution.py:84
  11.8 2.6 %collective-permute-start.4 = (bf16[20,208,128]{2,1,0:T(8,128)(2,1)}, bf16[20,208,128]{2,1,0:T(8,128)(2,1)}, u32[]{:S(2)}, u32[]{:S(2)}) collective-permute-start(bf16[20,208,128]{2,1,0:T(8,128)(2,1)} %get-tuple-element.5), channel_id=1, source_target_pairs={{0,4},{4,8},{8,12},{12,16},{16,20},{20,24},{24,28},{28,0},{1,5},{5... | collective-permute-start | bytes 3194888 | tf_op jit(solution)/shard_map/ppermute | solution.py:21
  14.4 0.0 collective-permute-start.3
  15.0 0.0 copy-done.4
  15.0 0.1 broadcast_in_dim.59
  15.1 0.1 abs.20
  15.3 0.8 %fusion.1 = (f32[13]{0:T(128)S(1)}, f32[13]{0:T(128)S(1)}, f32[13]{0:T(128)S(1)}, f32[13]{0:T(128)S(1)}) fusion(f32[4,4,13]{2,1,0:T(4,128)} %param.13, s32[]{:T(128)S(6)} %select_n.48, s32[]{:T(128)S(6)} %select_n.52, s32[]{:T(128)S(6)} %select_n.58, s32[]{:T(128)S(6)} %select_n.55), kind=kLoop, calls=%fused_computation.15 | loop fusion | bytes 432 | tf_op jit(solution)/shard_map/mul | solution.py:103
  16.8 0.1 pad.5.clone
  16.9 0.0 collective-permute-done.1
  16.9 0.0 collective-permute-done
  16.9 0.0 collective-permute-done.2
  16.9 0.1 multiply_add_fusion
  17.0 0.1 maximum_maximum_fusion.pk_ref
  17.0 1.7 %collective-permute-start.6 = (f32[16,128]{1,0:T(8,128)S(1)}, f32[16,128]{1,0:T(8,128)S(1)}, u32[]{:S(2)}, u32[]{:S(2)}) collective-permute-start(f32[16,128]{1,0:T(8,128)S(1)} %maximum_maximum_fusion.pk_ref), channel_id=1, source_target_pairs={{0,4},{4,8},{8,12},{12,16},{16,20},{20,24},{24,28},{28,0},{1,5},{5... | collective-permute-start | bytes 24584 | tf_op jit(solution)/shard_map/ppermute | solution.py:21
  18.8 0.0 collective-permute-start.5
  18.8 0.1 pad_maximum_fusion.1.sc_ref
  18.9 0.2 broadcast_in_dim.60.col_ref
  19.0 0.0 copy-done.1
  19.0 0.0 copy-done.2
  19.0 6.5 %shard_map.100.part_ref = f32[2,10,400,128]{3,2,1,0:T(8,128)} custom-call(f32[32]{0:T(128)S(1)} %pad_maximum_fusion.1.sc_ref, s32[2]{0:T(128)S(1)} %bitcast.27, bf16[20,400,128]{2,1,0:T(8,128)(2,1)S(1)} %bitcast.25, bf16[20,400,128]{2,1,0:T(8,128)(2,1)S(1)} %bitcast.26, bf16[20,200,128]{2,1,0:T(8,128)(2,1)S(1)} %copy-done.1, ...), custom_call_target="tpu_custom_call" | custom-call | tf_op jit(solution)/shard_map/pallas_call | solution.py:241
  25.5 10.8 %collective-permute-done.6.pp_ref = f32[16,128]{1,0:T(8,128)S(1)} collective-permute-done((f32[16,128]{1,0:T(8,128)S(1)}, f32[16,128]{1,0:T(8,128)S(1)}, u32[]{:S(2)}, u32[]{:S(2)}) %collective-permute-start.6) | collective-permute-done | bytes 8224 | tf_op jit(solution)/shard_map/ppermute | solution.py:21
  36.3 3.4 %collective-permute-done.5.pn_ref = f32[16,128]{1,0:T(8,128)S(1)} collective-permute-done((f32[16,128]{1,0:T(8,128)S(1)}, f32[16,128]{1,0:T(8,128)S(1)}, u32[]{:S(2)}, u32[]{:S(2)}) %collective-permute-start.5) | collective-permute-done | bytes 8224 | tf_op jit(solution)/shard_map/ppermute | solution.py:21
  39.8 0.0 collective-permute-done.4.prv_ref
  39.8 0.0 collective-permute-done.3.nxt_ref
  39.8 6.7 %shard_map.101 = bf16[20,400,128]{2,1,0:T(8,128)(2,1)} custom-call(f32[32]{0:T(128)S(1)} %pad_maximum_fusion.1.sc_ref, f32[2,10,400,128]{3,2,1,0:T(8,128)} %shard_map.100.part_ref, bf16[20,208,128]{2,1,0:T(8,128)(2,1)} %collective-permute-done.3.nxt_ref, bf16[20,208,128]{2,1,0:T(8,128)(2,1)} %collective-permute-done.4.prv_ref, ...), custom_call_target="tpu_custom_call" | custom-call | tf_op jit(solution)/shard_map/pallas_call | solution.py:320
  (7 shorter events, 0.1 us)
Async XLA Ops:
  1.5 1.8 %copy-start.3 = (bf16[39,8000]{1,0:T(8,128)(2,1)S(1)}, bf16[39,8000]{1,0:T(8,128)(2,1)}, u32[]{:S(2)}) copy-start(bf16[39,8000]{1,0:T(8,128)(2,1)} %constant.139.clone) | copy-start | bytes 1872004
  3.3 7.0 %copy-start = (bf16[1,400,20,128]{3,1,2,0:T(8,128)(2,1)S(1)}, bf16[1,400,20,128]{3,1,2,0:T(8,128)(2,1)}, u32[]{:S(2)}) copy-start(bf16[1,400,20,128]{3,1,2,0:T(8,128)(2,1)} %param.10) | copy-start | bytes 6144004
  3.8 13.0 %collective-permute-start.1 = (f32[13,128]{1,0:T(8,128)S(1)}, f32[13,128]{1,0:T(8,128)S(1)}, u32[]{:S(2)}, u32[]{:S(2)}) collective-permute-start(f32[13,128]{1,0:T(8,128)S(1)} %slice_add_fusion), channel_id=1, source_target_pairs={{0,2},{1,3},{2,0},{3,1},{4,6},{5,7},{6,4},{7,5},{8,10},{9,11},{10,... | collective-permute-start | bytes 19976 | tf_op jit(solution)/shard_map/ppermute | solution.py:21
  7.0 9.8 %collective-permute-start = (f32[13,128]{1,0:T(8,128)S(1)}, f32[13,128]{1,0:T(8,128)S(1)}, u32[]{:S(2)}, u32[]{:S(2)}) collective-permute-start(f32[13,128]{1,0:T(8,128)S(1)} %slice_add_fusion), channel_id=1, source_target_pairs={{0,1},{1,2},{2,3},{3,0},{4,5},{5,6},{6,7},{7,4},{8,9},{9,10},{10,1... | collective-permute-start | bytes 19976 | tf_op jit(solution)/shard_map/ppermute | solution.py:21
  8.3 8.6 %collective-permute-start.2 = (f32[13,128]{1,0:T(8,128)S(1)}, f32[13,128]{1,0:T(8,128)S(1)}, u32[]{:S(2)}, u32[]{:S(2)}) collective-permute-start(f32[13,128]{1,0:T(8,128)S(1)} %slice_add_fusion), channel_id=1, source_target_pairs={{0,3},{1,0},{2,1},{3,2},{4,7},{5,4},{6,5},{7,6},{8,11},{9,8},{10,9... | collective-permute-start | bytes 19976 | tf_op jit(solution)/shard_map/ppermute | solution.py:21
  10.3 4.7 %copy-start.4 = (f32[20]{0:T(128)S(1)}, f32[20]{0:T(128)}, u32[]{:S(2)}) copy-start(f32[20]{0:T(128)} %constant.140.clone) | copy-start | bytes 244
  10.3 8.7 %copy-start.1 = (bf16[20,200,128]{2,1,0:T(8,128)(2,1)S(1)}, bf16[20,200,128]{2,1,0:T(8,128)(2,1)}, u32[]{:S(2)}) copy-start(bf16[20,200,128]{2,1,0:T(8,128)(2,1)} %constant.141.clone.rec_lo.rec_hi.rec_ref) | copy-start | bytes 3072004
  10.3 8.7 %copy-start.2 = (s32[2,1]{0,1:T(1,128)S(1)}, s32[2,1]{0,1:T(1,128)}, u32[]{:S(2)}) copy-start(s32[2,1]{0,1:T(1,128)} %param.16) | copy-start | bytes 28
  11.8 28.0 %collective-permute-start.4 = (bf16[20,208,128]{2,1,0:T(8,128)(2,1)}, bf16[20,208,128]{2,1,0:T(8,128)(2,1)}, u32[]{:S(2)}, u32[]{:S(2)}) collective-permute-start(bf16[20,208,128]{2,1,0:T(8,128)(2,1)} %get-tuple-element.5), channel_id=1, source_target_pairs={{0,4},{4,8},{8,12},{12,16},{16,20},{20,24},{24,28},{28,0},{1,5},{5... | collective-permute-start | bytes 3194888 | tf_op jit(solution)/shard_map/ppermute | solution.py:21
  14.4 25.4 %collective-permute-start.3 = (bf16[20,208,128]{2,1,0:T(8,128)(2,1)}, bf16[20,208,128]{2,1,0:T(8,128)(2,1)}, u32[]{:S(2)}, u32[]{:S(2)}) collective-permute-start(bf16[20,208,128]{2,1,0:T(8,128)(2,1)} %get-tuple-element.6), channel_id=1, source_target_pairs={{0,28},{4,0},{8,4},{12,8},{16,12},{20,16},{24,20},{28,24},{1,29},{... | collective-permute-start | bytes 3194888 | tf_op jit(solution)/shard_map/ppermute | solution.py:21
  17.0 19.3 %collective-permute-start.6 = (f32[16,128]{1,0:T(8,128)S(1)}, f32[16,128]{1,0:T(8,128)S(1)}, u32[]{:S(2)}, u32[]{:S(2)}) collective-permute-start(f32[16,128]{1,0:T(8,128)S(1)} %maximum_maximum_fusion.pk_ref), channel_id=1, source_target_pairs={{0,4},{4,8},{8,12},{12,16},{16,20},{20,24},{24,28},{28,0},{1,5},{5... | collective-permute-start | bytes 24584 | tf_op jit(solution)/shard_map/ppermute | solution.py:21
  18.8 21.0 %collective-permute-start.5 = (f32[16,128]{1,0:T(8,128)S(1)}, f32[16,128]{1,0:T(8,128)S(1)}, u32[]{:S(2)}, u32[]{:S(2)}) collective-permute-start(f32[16,128]{1,0:T(8,128)S(1)} %maximum_maximum_fusion.pk_ref), channel_id=1, source_target_pairs={{0,28},{4,0},{8,4},{12,8},{16,12},{20,16},{24,20},{28,24},{1,29},{... | collective-permute-start | bytes 24584 | tf_op jit(solution)/shard_map/ppermute | solution.py:21

commit v2 on v1

--- a/solution.py
+++ b/solution.py
@@ -80,8 +80,7 @@
 
     field_in = jnp.transpose(cotangent[0], (1, 0, 2))
     margin = (-half) % 16
-    upper_in = field_in[:, half - margin :, :]
-    lower_in = field_in[:, : half + margin, :]
+    upper_in, lower_in = split_halves(field_in, half - margin, half + margin)
     got_next = passed_along(upper_in, "space", -1)
     got_prev = passed_along(lower_in, "space", 1)
 
@@ -162,6 +161,28 @@
             at = side * (lanes // 2) + block * rows
             packed[:, :, at : at + moment_count] = parts[part][:, side * half : (side + 1) * half]
     return packed.astype(jnp.bfloat16)
+
+
+def split_halves(field_in, start, wide):
+    node_count, pair_count, cell_count = field_in.shape
+    group = 5 if node_count % 5 == 0 else 1
+
+    def kernel(x_ref, up_ref, lo_ref):
+        up_ref[...] = x_ref[:, start : start + wide, :]
+        lo_ref[...] = x_ref[:, :wide, :]
+
+    shape = jax.ShapeDtypeStruct((node_count, wide, cell_count), field_in.dtype)
+    return pl.pallas_call(
+        kernel,
+        grid=(node_count // group,),
+        in_specs=[pl.BlockSpec((group, pair_count, cell_count), lambda i: (i, 0, 0))],
+        out_specs=[
+            pl.BlockSpec((group, wide, cell_count), lambda i: (i, 0, 0)),
+            pl.BlockSpec((group, wide, cell_count), lambda i: (i, 0, 0)),
+        ],
+        out_shape=[shape, shape],
+        compiler_params=pltpu.CompilerParams(dimension_semantics=("arbitrary",)),
+    )(field_in)
 
 
 def cross_matrix(packet, moment_count, side):

time: 46.7 us -> 49.8 us (1.066)
  the two profiles are of different devices: /device:TPU:1 before, /device:TPU:0 now
where the time goes in v2:
time: 49.8 us; the launch traced here: 49.5 us
  Pallas kernels  16.9 us (34%)
  waiting for transfers between devices  14.1 us (28%)
  starting transfers between devices  11.7 us (23%)
  other arithmetic  3.58 us (7%)
  between operations  1.47 us (3%)
  local copies, waits for them, and re-layouts  1.28 us (3%)
    ppermute x7, waiting for transfers between devices, passed_along(): return lax.ppermute(value, axis, pairs)  14.1 us
    ppermute x7, starting transfers between devices, passed_along(): return lax.ppermute(value, axis, pairs)  11.7 us
    pallas_call x1, Pallas kernels, halo_kernel(): pl.pallas_call(kernel, grid=(blocks,), in_specs=in_specs, out_specs=pl.Bl...  6.66 us
    pallas_call x1, Pallas kernels, own_kernel(): pl.pallas_call(kernel, grid=(blocks,), in_specs=in_specs, out_specs=pl.Bl...  6.47 us
    pallas_call x1, Pallas kernels, split_halves(): pl.pallas_call(kernel, grid=(node_count // group,), in_specs=[pl.BlockSpe...  3.76 us
    mul x1, other arithmetic, on_device(): masked = field_in * keep.astype(jnp.bfloat16)  1.82 us
  transfers between devices with their start and end apart: 7, of which 1 were waited for; matrix products, arithmetic and copies ran while one was open for 3% of the time, Pallas kernels for 21%

profile of v2, /device:TPU:0, one launch (start us, length us, event | category | flops | bytes accessed | tf_op | source)
XLA Modules:
  0.0 49.5 jit_solution(3178888319533967303)
XLA Ops:
  0.0 0.7 %subtract_convert_fusion = (bf16[128]{0:T(256)(128)(2,1)S(1)}, f32[1,128]{1,0:T(1,128)S(1)}) fusion(s32[128]{0:T(128)} %param.14), kind=kLoop, calls=%fused_computation.21 | loop fusion | flops 384 | bytes 1280 | tf_op jit(solution)/shard_map/convert_element_type | solution.py:87
  0.7 0.7 %subtract_multiply_fusion = f32[128]{0:T(128)S(1)} fusion(s32[128]{0:T(128)} %param.15, s32[128]{0:T(128)} %param.14), kind=kLoop, calls=%fused_computation.20 | loop fusion | flops 640 | bytes 1536 | tf_op jit(solution)/shard_map/mul | solution.py:88
  1.3 0.1 select_convert_fusion
  1.5 0.0 copy-start.3
  1.5 1.8 %broadcast_multiply_fusion = bf16[20,400,128]{2,1,0:T(8,128)(2,1)S(1)} fusion(bf16[400,128]{1,0:T(8,128)(2,1)S(1)} %select_convert_fusion, bf16[1,400,20,128]{3,1,2,0:T(8,128)(2,1)} %param.10), kind=kLoop, calls=%fused_computation | loop fusion | flops 1024000 | bytes 4198400 | tf_op jit(solution)/shard_map/mul | solution.py:91
  3.3 0.0 copy-done.3
  3.3 0.0 copy-start.4
  3.3 0.5 fusion.6
  3.8 0.0 copy-start
  3.8 0.0 copy-start.1
  3.8 0.0 copy-start.2
  3.9 4.1 %collective-permute-start.1 = (f32[13,128]{1,0:T(8,128)S(1)}, f32[13,128]{1,0:T(8,128)S(1)}, u32[]{:S(2)}, u32[]{:S(2)}) collective-permute-start(f32[13,128]{1,0:T(8,128)S(1)} %slice_add_fusion), channel_id=1, source_target_pairs={{0,2},{1,3},{2,0},{3,1},{4,6},{5,7},{6,4},{7,5},{8,10},{9,11},{10,... | collective-permute-start | bytes 19976 | tf_op jit(solution)/shard_map/ppermute | solution.py:21
  8.0 1.6 %collective-permute-start = (f32[13,128]{1,0:T(8,128)S(1)}, f32[13,128]{1,0:T(8,128)S(1)}, u32[]{:S(2)}, u32[]{:S(2)}) collective-permute-start(f32[13,128]{1,0:T(8,128)S(1)} %slice_add_fusion), channel_id=1, source_target_pairs={{0,1},{1,2},{2,3},{3,0},{4,5},{5,6},{6,7},{7,4},{8,9},{9,10},{10,1... | collective-permute-start | bytes 19976 | tf_op jit(solution)/shard_map/ppermute | solution.py:21
  9.6 2.2 %collective-permute-start.2 = (f32[13,128]{1,0:T(8,128)S(1)}, f32[13,128]{1,0:T(8,128)S(1)}, u32[]{:S(2)}, u32[]{:S(2)}) collective-permute-start(f32[13,128]{1,0:T(8,128)S(1)} %slice_add_fusion), channel_id=1, source_target_pairs={{0,3},{1,0},{2,1},{3,2},{4,7},{5,4},{6,5},{7,6},{8,11},{9,8},{10,9... | collective-permute-start | bytes 19976 | tf_op jit(solution)/shard_map/ppermute | solution.py:21
  11.8 3.8 %shard_map.101 = (bf16[20,208,128]{2,1,0:T(8,128)(2,1)}, bf16[20,208,128]{2,1,0:T(8,128)(2,1)}) custom-call(bf16[20,400,128]{2,1,0:T(8,128)(2,1)} %bitcast.24), custom_call_target="tpu_custom_call" | custom-call | tf_op jit(solution)/shard_map/pallas_call | solution.py:175
  15.6 1.0 %collective-permute-start.3 = (bf16[20,208,128]{2,1,0:T(8,128)(2,1)}, bf16[20,208,128]{2,1,0:T(8,128)(2,1)}, u32[]{:S(2)}, u32[]{:S(2)}) collective-permute-start(bf16[20,208,128]{2,1,0:T(8,128)(2,1)} %get-tuple-element.7), channel_id=1, source_target_pairs={{0,28},{4,0},{8,4},{12,8},{16,12},{20,16},{24,20},{28,24},{1,29},{... | collective-permute-start | bytes 3194888 | tf_op jit(solution)/shard_map/ppermute | solution.py:21
  16.6 0.0 collective-permute-start.4
  17.3 0.0 copy-done.4
  17.3 0.1 broadcast_in_dim.59
  17.4 0.1 abs.20
  17.6 0.8 %fusion.1 = (f32[13]{0:T(128)S(1)}, f32[13]{0:T(128)S(1)}, f32[13]{0:T(128)S(1)}, f32[13]{0:T(128)S(1)}) fusion(f32[4,4,13]{2,1,0:T(4,128)} %param.13, s32[]{:T(128)S(6)} %select_n.48, s32[]{:T(128)S(6)} %select_n.52, s32[]{:T(128)S(6)} %select_n.58, s32[]{:T(128)S(6)} %select_n.55), kind=kLoop, calls=%fused_computation.15 | loop fusion | bytes 432 | tf_op jit(solution)/shard_map/mul | solution.py:102
  19.1 0.1 pad.5.clone
  19.1 0.0 collective-permute-done.1
  19.1 0.0 collective-permute-done
  19.1 0.0 collective-permute-done.2
  19.1 0.1 multiply_add_fusion
  19.2 0.1 maximum_maximum_fusion.pk_ref
  19.3 0.6 %collective-permute-start.6 = (f32[16,128]{1,0:T(8,128)S(1)}, f32[16,128]{1,0:T(8,128)S(1)}, u32[]{:S(2)}, u32[]{:S(2)}) collective-permute-start(f32[16,128]{1,0:T(8,128)S(1)} %maximum_maximum_fusion.pk_ref), channel_id=1, source_target_pairs={{0,4},{4,8},{8,12},{12,16},{16,20},{20,24},{24,28},{28,0},{1,5},{5... | collective-permute-start | bytes 24584 | tf_op jit(solution)/shard_map/ppermute | solution.py:21
  19.9 2.1 %collective-permute-start.5 = (f32[16,128]{1,0:T(8,128)S(1)}, f32[16,128]{1,0:T(8,128)S(1)}, u32[]{:S(2)}, u32[]{:S(2)}) collective-permute-start(f32[16,128]{1,0:T(8,128)S(1)} %maximum_maximum_fusion.pk_ref), channel_id=1, source_target_pairs={{0,28},{4,0},{8,4},{12,8},{16,12},{20,16},{24,20},{28,24},{1,29},{... | collective-permute-start | bytes 24584 | tf_op jit(solution)/shard_map/ppermute | solution.py:21
  22.0 0.1 pad_maximum_fusion.1.sc_ref
  22.1 0.2 broadcast_in_dim.60.col_ref
  22.2 0.0 copy-done
  22.3 0.0 copy-done.1
  22.3 0.0 copy-done.2
  22.3 6.5 %shard_map.100.part_ref = f32[2,10,400,128]{3,2,1,0:T(8,128)} custom-call(f32[32]{0:T(128)S(1)} %pad_maximum_fusion.1.sc_ref, s32[2]{0:T(128)S(1)} %bitcast.27, bf16[20,400,128]{2,1,0:T(8,128)(2,1)S(1)} %bitcast.25, bf16[20,400,128]{2,1,0:T(8,128)(2,1)S(1)} %bitcast.26, bf16[20,200,128]{2,1,0:T(8,128)(2,1)S(1)} %copy-done.1, ...), custom_call_target="tpu_custom_call" | custom-call | tf_op jit(solution)/shard_map/pallas_call | solution.py:262
  28.7 14.1 %collective-permute-done.6.pp_ref = f32[16,128]{1,0:T(8,128)S(1)} collective-permute-done((f32[16,128]{1,0:T(8,128)S(1)}, f32[16,128]{1,0:T(8,128)S(1)}, u32[]{:S(2)}, u32[]{:S(2)}) %collective-permute-start.6) | collective-permute-done | bytes 8224 | tf_op jit(solution)/shard_map/ppermute | solution.py:21
  42.8 0.0 collective-permute-done.5.pn_ref
  42.8 0.0 collective-permute-done.3.nxt_ref
  42.8 0.0 collective-permute-done.4.prv_ref
  42.8 6.7 %shard_map.102 = bf16[20,400,128]{2,1,0:T(8,128)(2,1)} custom-call(f32[32]{0:T(128)S(1)} %pad_maximum_fusion.1.sc_ref, f32[2,10,400,128]{3,2,1,0:T(8,128)} %shard_map.100.part_ref, bf16[20,208,128]{2,1,0:T(8,128)(2,1)} %collective-permute-done.3.nxt_ref, bf16[20,208,128]{2,1,0:T(8,128)(2,1)} %collective-permute-done.4.prv_ref, ...), custom_call_target="tpu_custom_call" | custom-call | tf_op jit(solution)/shard_map/pallas_call | solution.py:341
  (7 shorter events, 0.1 us)
Async XLA Ops:
  1.5 1.8 %copy-start.3 = (bf16[39,8000]{1,0:T(8,128)(2,1)S(1)}, bf16[39,8000]{1,0:T(8,128)(2,1)}, u32[]{:S(2)}) copy-start(bf16[39,8000]{1,0:T(8,128)(2,1)} %constant.139.clone) | copy-start | bytes 1872004
  3.3 14.0 %copy-start.4 = (f32[20]{0:T(128)S(1)}, f32[20]{0:T(128)}, u32[]{:S(2)}) copy-start(f32[20]{0:T(128)} %constant.140.clone) | copy-start | bytes 244
  3.8 18.4 %copy-start = (bf16[1,400,20,128]{3,1,2,0:T(8,128)(2,1)S(1)}, bf16[1,400,20,128]{3,1,2,0:T(8,128)(2,1)}, u32[]{:S(2)}) copy-start(bf16[1,400,20,128]{3,1,2,0:T(8,128)(2,1)} %param.10) | copy-start | bytes 6144004
  3.8 18.4 %copy-start.1 = (bf16[20,200,128]{2,1,0:T(8,128)(2,1)S(1)}, bf16[20,200,128]{2,1,0:T(8,128)(2,1)}, u32[]{:S(2)}) copy-start(bf16[20,200,128]{2,1,0:T(8,128)(2,1)} %constant.141.clone.rec_lo.rec_hi.rec_ref) | copy-start | bytes 3072004
  3.8 18.4 %copy-start.2 = (s32[2,1]{0,1:T(1,128)S(1)}, s32[2,1]{0,1:T(1,128)}, u32[]{:S(2)}) copy-start(s32[2,1]{0,1:T(1,128)} %param.16) | copy-start | bytes 28
  3.9 15.3 %collective-permute-start.1 = (f32[13,128]{1,0:T(8,128)S(1)}, f32[13,128]{1,0:T(8,128)S(1)}, u32[]{:S(2)}, u32[]{:S(2)}) collective-permute-start(f32[13,128]{1,0:T(8,128)S(1)} %slice_add_fusion), channel_id=1, source_target_pairs={{0,2},{1,3},{2,0},{3,1},{4,6},{5,7},{6,4},{7,5},{8,10},{9,11},{10,... | collective-permute-start | bytes 19976 | tf_op jit(solution)/shard_map/ppermute | solution.py:21
  8.0 11.1 %collective-permute-start = (f32[13,128]{1,0:T(8,128)S(1)}, f32[13,128]{1,0:T(8,128)S(1)}, u32[]{:S(2)}, u32[]{:S(2)}) collective-permute-start(f32[13,128]{1,0:T(8,128)S(1)} %slice_add_fusion), channel_id=1, source_target_pairs={{0,1},{1,2},{2,3},{3,0},{4,5},{5,6},{6,7},{7,4},{8,9},{9,10},{10,1... | collective-permute-start | bytes 19976 | tf_op jit(solution)/shard_map/ppermute | solution.py:21
  9.6 9.6 %collective-permute-start.2 = (f32[13,128]{1,0:T(8,128)S(1)}, f32[13,128]{1,0:T(8,128)S(1)}, u32[]{:S(2)}, u32[]{:S(2)}) collective-permute-start(f32[13,128]{1,0:T(8,128)S(1)} %slice_add_fusion), channel_id=1, source_target_pairs={{0,3},{1,0},{2,1},{3,2},{4,7},{5,4},{6,5},{7,6},{8,11},{9,8},{10,9... | collective-permute-start | bytes 19976 | tf_op jit(solution)/shard_map/ppermute | solution.py:21
  15.6 27.2 %collective-permute-start.3 = (bf16[20,208,128]{2,1,0:T(8,128)(2,1)}, bf16[20,208,128]{2,1,0:T(8,128)(2,1)}, u32[]{:S(2)}, u32[]{:S(2)}) collective-permute-start(bf16[20,208,128]{2,1,0:T(8,128)(2,1)} %get-tuple-element.7), channel_id=1, source_target_pairs={{0,28},{4,0},{8,4},{12,8},{16,12},{20,16},{24,20},{28,24},{1,29},{... | collective-permute-start | bytes 3194888 | tf_op jit(solution)/shard_map/ppermute | solution.py:21
  16.6 26.2 %collective-permute-start.4 = (bf16[20,208,128]{2,1,0:T(8,128)(2,1)}, bf16[20,208,128]{2,1,0:T(8,128)(2,1)}, u32[]{:S(2)}, u32[]{:S(2)}) collective-permute-start(bf16[20,208,128]{2,1,0:T(8,128)(2,1)} %get-tuple-element.8), channel_id=1, source_target_pairs={{0,4},{4,8},{8,12},{12,16},{16,20},{20,24},{24,28},{28,0},{1,5},{5... | collective-permute-start | bytes 3194888 | tf_op jit(solution)/shard_map/ppermute | solution.py:21
  19.3 23.5 %collective-permute-start.6 = (f32[16,128]{1,0:T(8,128)S(1)}, f32[16,128]{1,0:T(8,128)S(1)}, u32[]{:S(2)}, u32[]{:S(2)}) collective-permute-start(f32[16,128]{1,0:T(8,128)S(1)} %maximum_maximum_fusion.pk_ref), channel_id=1, source_target_pairs={{0,4},{4,8},{8,12},{12,16},{16,20},{20,24},{24,28},{28,0},{1,5},{5... | collective-permute-start | bytes 24584 | tf_op jit(solution)/shard_map/ppermute | solution.py:21
  19.9 22.9 %collective-permute-start.5 = (f32[16,128]{1,0:T(8,128)S(1)}, f32[16,128]{1,0:T(8,128)S(1)}, u32[]{:S(2)}, u32[]{:S(2)}) collective-permute-start(f32[16,128]{1,0:T(8,128)S(1)} %maximum_maximum_fusion.pk_ref), channel_id=1, source_target_pairs={{0,28},{4,0},{8,4},{12,8},{16,12},{20,16},{24,20},{28,24},{1,29},{... | collective-permute-start | bytes 24584 | tf_op jit(solution)/shard_map/ppermute | solution.py:21
